TPU v7x, 512 devices: a whole 4x8x8 slice. The times are simulated.
512 devices in a mesh: dp: 8 (over z), expert: 64 (over y, x, core).
Axes of the slice: x: 4, y: 8, z: 8, core: 2. Of those that a mesh axis runs over, the one named last changes fastest.
Arguments:
- tokens: bfloat16 [65536, 1024], P(('dp', 'expert')), may hold values from -6 to 6
- expert_ids: int32 [65536, 4], P(('dp', 'expert')), may hold values from 0 to 63, all different within a row; in each aligned block of 128 rows (0 to 127, 128 to 255, ...) at most 16 rows name the same one
- gate_probs: float32 [65536, 4], P(('dp', 'expert')), may hold values from 0.05 to 1
- gate_up: bfloat16 [64, 1024, 768], P('expert', 'dp'), may hold values from -0.1875 to 0.1875
- down_proj: bfloat16 [64, 384, 1024], P('expert', None, 'dp'), may hold values from -0.3125 to 0.3125
- cotangent: bfloat16 [65536, 1024], P(('dp', 'expert')), may hold values from -0.75 to 0.75
Outputs:
- moe_out: bfloat16 [65536, 1024], P(('dp', 'expert'))
- token_grads: bfloat16 [65536, 1024], P(('dp', 'expert'))
- gate_grads: float32 [65536, 4], P(('dp', 'expert'))
- gate_up_grads: float32 [64, 1024, 768], P('expert', 'dp')
- down_grads: float32 [64, 384, 1024], P('expert', None, 'dp')
Inputs may be any that keep to these rules, and one draw needn't show every extreme that they name: `expert_ids`: each row names 4 different experts. Among the rows of one device no expert is named more than 16 times, and in every draw some device names some expert exactly 16 times.
All inputs are finite; a program needn't handle non-finite values.
Results may differ from a plain program's by a relative error of at most 0.012.
Values may be sent and summed in bfloat16 or wider, within the bound.
No kernel may reach another device: no remote copies, remote signals or barrier semaphores. Data moves between devices by JAX's collectives and lax.ppermute only.
A program may use at most 64 MiB of HBM per device.

v0:
```python
import jax
import jax.numpy as jnp
from jax import lax
from jax.sharding import PartitionSpec as P


def expert_rows(rows_in, grad_rows, weight_in, weight_out_t):
    hidden_width = weight_out_t.shape[1]
    contract_last = (((1,), (1,)), ((), ()))
    contract_first = (((0,), (0,)), ((), ()))
    pre_act = jnp.dot(rows_in, weight_in, preferred_element_type=jnp.float32)
    pre_gate = pre_act[:, :hidden_width]
    up_value = pre_act[:, hidden_width:]
    act = jax.nn.silu(pre_gate)
    hidden = (act * up_value).astype(jnp.bfloat16)
    expert_out = lax.dot_general(
        hidden, weight_out_t, contract_last, preferred_element_type=jnp.float32
    ).astype(jnp.bfloat16)
    grad_hidden = jnp.dot(grad_rows, weight_out_t, preferred_element_type=jnp.float32)
    sigmoid_value = jax.nn.sigmoid(pre_gate)
    grad_gate = grad_hidden * up_value * sigmoid_value * (1.0 + pre_gate * (1.0 - sigmoid_value))
    grad_up = grad_hidden * act
    grad_pre = jnp.concatenate([grad_gate, grad_up], axis=1).astype(jnp.bfloat16)
    grad_in = lax.dot_general(
        grad_pre, weight_in, contract_last, preferred_element_type=jnp.float32
    ).astype(jnp.bfloat16)
    weight_in_grad = lax.dot_general(
        rows_in, grad_pre, contract_first, preferred_element_type=jnp.float32
    ).astype(jnp.bfloat16)
    weight_out_grad_t = lax.dot_general(
        grad_rows, hidden, contract_first, preferred_element_type=jnp.float32
    ).astype(jnp.bfloat16)
    return (expert_out, grad_in, weight_in_grad, weight_out_grad_t)


def local(tokens, expert_ids, gate_probs, gate_up, down_proj, cotangent):
    token_count, top_count = expert_ids.shape
    width = tokens.shape[1]
    expert_count = lax.axis_size("expert")
    capacity = 2 * token_count * top_count // expert_count
    route_count = token_count * top_count
    slot_count = expert_count * capacity
    gate_width = gate_up.shape[2]
    weights = jnp.concatenate([gate_up[0], down_proj[0].T], axis=1)
    weights = lax.all_gather(weights, "dp", axis=0, tiled=True)
    weight_in = weights[:, :gate_width]
    weight_out_t = weights[:, gate_width:]
    flat_ids = expert_ids.reshape(route_count)
    onehot = (flat_ids[:, None] == jnp.arange(expert_count, dtype=jnp.int32)[None, :]).astype(
        jnp.int32
    )
    slot_index = jnp.sum((jnp.cumsum(onehot, axis=0) - onehot) * onehot, axis=1)
    position = (flat_ids * capacity + slot_index).reshape(token_count, top_count)
    slot_range = jnp.arange(slot_count, dtype=jnp.int32)
    hits = position[None, :, :] == slot_range[:, None, None]
    select = jnp.any(hits, axis=2)
    weighted = jnp.sum(jnp.where(hits, gate_probs[None, :, :], 0.0), axis=2)
    slot_probs = jnp.sum(weighted, axis=1)
    select_rows = select.astype(jnp.bfloat16)
    both = jnp.concatenate([tokens, cotangent], axis=1)
    gathered = jnp.dot(select_rows, both, preferred_element_type=jnp.float32)
    send_tokens = gathered[:, :width].astype(jnp.bfloat16)
    slot_cot = gathered[:, width:]
    send_grads = (slot_probs[:, None] * slot_cot).astype(jnp.bfloat16)
    send = jnp.concatenate([send_tokens, send_grads], axis=1)
    recv = lax.all_to_all(send, "expert", split_axis=0, concat_axis=0, tiled=True)
    rows_in = recv[:, :width]
    grad_rows = recv[:, width:]
    expert_out, grad_in, weight_in_grad, weight_out_grad_t = expert_rows(
        rows_in, grad_rows, weight_in, weight_out_t
    )
    back = lax.all_to_all(
        jnp.concatenate([expert_out, grad_in], axis=1),
        "expert",
        split_axis=0,
        concat_axis=0,
        tiled=True,
    )
    grads = lax.psum_scatter(
        jnp.concatenate([weight_in_grad, weight_out_grad_t], axis=1),
        "dp",
        scatter_dimension=0,
        tiled=True,
    ).astype(jnp.float32)
    sum_in = grads[None, :, :gate_width]
    sum_out = grads[:, gate_width:].T[None]
    back_out = back[:, :width].astype(jnp.float32)
    back_grad = back[:, width:]
    moe_out = lax.dot_general(
        weighted,
        back_out,
        (((0,), (0,)), ((), ())),
        precision=lax.Precision.HIGHEST,
        preferred_element_type=jnp.float32,
    ).astype(jnp.bfloat16)
    token_grads = lax.dot_general(
        select_rows, back_grad, (((0,), (0,)), ((), ())), preferred_element_type=jnp.float32
    ).astype(jnp.bfloat16)
    slot_gate = jnp.sum(slot_cot * back_out, axis=1)
    gate_grads = slot_gate[position]
    return (moe_out, token_grads, gate_grads, sum_in, sum_out)


def solution(mesh):
    return jax.shard_map(
        local,
        mesh=mesh,
        in_specs=(
            P(("dp", "expert"), None),
            P(("dp", "expert"), None),
            P(("dp", "expert"), None),
            P("expert", "dp", None),
            P("expert", None, "dp"),
            P(("dp", "expert"), None),
        ),
        out_specs=(
            P(("dp", "expert"), None),
            P(("dp", "expert"), None),
            P(("dp", "expert"), None),
            P("expert", "dp", None),
            P("expert", None, "dp"),
        ),
        check_vma=False,
    )
```

profile of v0, /device:TPU:2, one launch (start us, length us, event | category | flops | bytes accessed | tf_op | source)
XLA Modules:
  0.0 268.4 jit_solution(10926325315860447653)
XLA Ops:
  7.2 0.8 copy.46
  8.0 0.1 eq.42
  8.1 0.1 eq.38
  8.2 1.2 reduce-window.6
  9.4 0.2 slice_reduce_fusion
  9.7 0.1 fusion.36
  9.8 0.1 reduce_sum.39
  9.9 0.1 copy.49
  10.0 0.7 compare_select_fusion
  10.7 0.4 fusion.2
  11.0 1.0 select_reduce_fusion
  12.1 2.3 fusion.30
  14.3 0.0 copy-start
  14.3 0.3 slice.115
  14.7 2.9 %copy-done = f32[1024,2048]{1,0:T(8,128)} copy-done((f32[1024,2048]{1,0:T(8,128)}, f32[1024,2048]{1,0:T(8,128)S(1)}, u32[]{:S(2)}) %copy-start) | copy-done | bytes 8388632
  17.6 0.3 multiply_convert_fusion
  17.9 2.4 pad_maximum_fusion
  20.3 0.0 copy-start.2
  20.3 0.0 copy-start.1
  20.3 11.1 %all-to-all-start = ((bf16[64,16,2048]{2,1,0:T(8,128)(2,1)}), bf16[64,16,2048]{2,1,0:T(8,128)(2,1)}, u32[]{:S(2)}, u32[]{:S(2)}) async-start(bf16[64,16,2048]{2,1,0:T(8,128)(2,1)} %bitcast.40), calls=%async_computation | async-start | bytes 8388608 | tf_op jit(solution)/shard_map/all_to_all | solution.py:66
  31.3 0.0 all-gather.2.cloned.1.call-start
  31.4 0.0 copy-done.2
  31.4 0.1 copy.50
  31.5 0.0 copy-done.1
  31.5 0.7 pad_maximum_fusion.6
  32.3 0.0 all-gather.2.cloned.1.call-update
  32.3 51.1 %all-gather.2.cloned.1.call-done = bf16[1024,1152]{1,0:T(8,128)(2,1)} async-done(((bf16[128,1152]{1,0:T(8,128)(2,1)}), bf16[1024,1152]{1,0:T(8,128)(2,1)}) %all-gather.2.cloned.1.call-update) | async-done | bytes 2359312 | tf_op jit(solution)/shard_map/all_gather | solution.py:45
  83.4 44.2 %all-to-all-done = bf16[64,16,2048]{2,1,0:T(8,128)(2,1)} async-done(((bf16[64,16,2048]{2,1,0:T(8,128)(2,1)}), bf16[64,16,2048]{2,1,0:T(8,128)(2,1)}, u32[]{:S(2)}, u32[]{:S(2)}) %all-to-all-start) | async-done | bytes 4194336 | tf_op jit(solution)/shard_map/all_to_all | solution.py:66
  127.5 0.0 copy-start.3
  127.5 4.1 %fusion.11 = f32[1024,768]{0,1:T(8,128)S(1)} fusion(bf16[1024,2048]{1,0:T(8,128)(2,1)} %bitcast.2, bf16[1024,1152]{1,0:T(8,128)(2,1)} %all-gather.2.cloned.1.call-done), kind=kOutput, calls=%fused_computation.23 | convolution fusion | flops 1610612736 | bytes 6815744 | tf_op jit(solution)/shard_map/dot_general | solution.py:11
  131.6 0.0 copy-done.3
  131.6 3.3 %multiply_convert_fusion.2 = (bf16[1024,384]{0,1:T(8,128)(2,1)S(1)}, bf16[1024,384]{0,1:T(8,128)(2,1)S(1)}, bf16[1024,384]{0,1:T(8,128)(2,1)S(1)}) fusion(f32[1024,768]{0,1:T(8,128)S(1)} %fusion.11, bf16[1024,1152]{1,0:T(8,128)(2,1)S(1)} %copy-done.3, bf16[1024,2048]{1,0:T(8,128)(2,1)} %bitcast.2), kind=kOutput, calls=%fused_computation.28 | convolution fusion | flops 811204608 | bytes 8388608 | tf_op jit(solution)/shard_map/dot_general | solution.py:19
  134.9 1.3 convolution_convert_fusion
  136.1 1.8 convolution_convert_fusion.1
  137.9 2.4 pad_maximum_fusion.1
  140.3 6.5 %copy.51 = bf16[1024,2048]{1,0:T(8,128)(2,1)} copy(bf16[1024,2048]{0,1:T(8,128)(2,1)} %pad_maximum_fusion.1) | data formatting | bytes 8388608 | tf_op jit(solution)/shard_map/concatenate | solution.py:73
  146.8 5.9 %all-to-all-start.1 = ((bf16[64,16,2048]{2,1,0:T(8,128)(2,1)}), bf16[64,16,2048]{2,1,0:T(8,128)(2,1)}, u32[]{:S(2)}, u32[]{:S(2)}) async-start(bf16[64,16,2048]{2,1,0:T(8,128)(2,1)} %bitcast.39), calls=%async_computation.1 | async-start | bytes 8388608 | tf_op jit(solution)/shard_map/all_to_all | solution.py:72
  152.7 0.0 reduce-scatter.4.cloned.1.call-start
  152.8 2.6 fusion.17
  155.4 3.4 %fusion.13 = bf16[1024,768]{0,1:T(8,128)(2,1)S(1)} fusion(bf16[1024,2048]{1,0:T(8,128)(2,1)} %bitcast.2, bf16[1024,384]{0,1:T(8,128)(2,1)S(1)} %get-tuple-element.35, bf16[1024,384]{0,1:T(8,128)(2,1)S(1)} %get-tuple-element.34), kind=kOutput, calls=%fused_computation.25 | convolution fusion | flops 1614544896 | bytes 5242880 | tf_op jit(solution)/shard_map/dot_general | solution.py:27
  158.7 0.2 pad_maximum_fusion.2
  159.0 2.5 copy.55
  161.5 0.0 reduce-scatter.4.cloned.1.call-update
  161.5 0.1 copy.52
  161.6 0.1 reshape.45
  161.8 50.8 %reduce-scatter.4.cloned.1.call-done = bf16[128,1152]{1,0:T(8,128)(2,1)} async-done(((bf16[1024,1152]{1,0:T(8,128)(2,1)}), bf16[128,1152]{1,0:T(8,128)(2,1)}) %reduce-scatter.4.cloned.1.call-update) | async-done | bytes 294928
  212.6 1.2 copy.56
  213.8 0.9 copy.54
  214.8 0.7 slice_bitcast_fusion.1
  215.5 33.5 %all-to-all-done.1 = bf16[64,16,2048]{2,1,0:T(8,128)(2,1)} async-done(((bf16[64,16,2048]{2,1,0:T(8,128)(2,1)}), bf16[64,16,2048]{2,1,0:T(8,128)(2,1)}, u32[]{:S(2)}, u32[]{:S(2)}) %all-to-all-start.1) | async-done | bytes 4194336 | tf_op jit(solution)/shard_map/all_to_all | solution.py:72
  248.9 3.3 %multiply_reduce_fusion = f32[1024]{0:T(1024)S(1)} fusion(f32[1024,2048]{1,0:T(8,128)} %copy-done, bf16[1024,2048]{1,0:T(8,128)(2,1)} %bitcast.7), kind=kLoop, calls=%fused_computation.4 | loop fusion | flops 3144704 | bytes 6295552 | tf_op jit(solution)/shard_map/reduce_sum | solution.py:99
  252.3 2.8 %fusion.25 = bf16[128,1024]{1,0:T(8,128)(2,1)} fusion(pred[1024,128]{1,0:T(8,128)(4,1)S(1)} %fusion.2, bf16[1024,2048]{1,0:T(8,128)(2,1)} %bitcast.7), kind=kOutput, calls=%fused_computation.36 | convolution fusion | flops 268566528 | bytes 2490368 | tf_op jit(solution)/shard_map/dot_general | solution.py:96
  255.1 2.3 gather_fusion
  257.4 0.1 reshape.44
  257.5 0.7 copy.53
  258.1 3.4 %fusion.22 = bf16[128,1024]{1,0:T(8,128)(2,1)} fusion(f32[1024,128]{1,0:T(8,128)S(1)} %get-tuple-element.31, bf16[1024,2048]{1,0:T(8,128)(2,1)} %bitcast.7), kind=kOutput, calls=%fused_computation.35 | convolution fusion | flops 1610743808 | bytes 2883584 | tf_op jit(solution)/shard_map/dot_general | solution.py:89
  (6 shorter events, 0.1 us)
Async XLA Ops:
  14.3 3.2 %copy-start = (f32[1024,2048]{1,0:T(8,128)}, f32[1024,2048]{1,0:T(8,128)S(1)}, u32[]{:S(2)}) copy-start(f32[1024,2048]{1,0:T(8,128)S(1)} %fusion.30) | copy-start | bytes 25165828
  20.3 11.1 %copy-start.2 = (bf16[1,384,128]{2,1,0:T(8,128)(2,1)S(1)}, bf16[1,384,128]{2,1,0:T(8,128)(2,1)}, u32[]{:S(2)}) copy-start(bf16[1,384,128]{2,1,0:T(8,128)(2,1)} %param.10) | copy-start | bytes 294916
  20.3 11.2 %copy-start.1 = (bf16[1,128,768]{2,1,0:T(8,128)(2,1)S(1)}, bf16[1,128,768]{2,1,0:T(8,128)(2,1)}, u32[]{:S(2)}) copy-start(bf16[1,128,768]{2,1,0:T(8,128)(2,1)} %param.9) | copy-start | bytes 589828
  20.3 107.3 %all-to-all-start = ((bf16[64,16,2048]{2,1,0:T(8,128)(2,1)}), bf16[64,16,2048]{2,1,0:T(8,128)(2,1)}, u32[]{:S(2)}, u32[]{:S(2)}) async-start(bf16[64,16,2048]{2,1,0:T(8,128)(2,1)} %bitcast.40), calls=%async_computation | async-start | bytes 8388608 | tf_op jit(solution)/shard_map/all_to_all | solution.py:66
  31.3 52.0 %all-gather.2.cloned.1.call-start = ((), (), s32[]{:S(2)}) async-start(), calls=%async_computation.3 | async-start | bytes 2654208 | tf_op jit(solution)/shard_map/all_gather | solution.py:45
  127.5 4.1 %copy-start.3 = (bf16[1024,1152]{1,0:T(8,128)(2,1)S(1)}, bf16[1024,1152]{1,0:T(8,128)(2,1)}, u32[]{:S(2)}) copy-start(bf16[1024,1152]{1,0:T(8,128)(2,1)} %all-gather.2.cloned.1.call-done) | copy-start | bytes 7077892
  146.8 102.1 %all-to-all-start.1 = ((bf16[64,16,2048]{2,1,0:T(8,128)(2,1)}), bf16[64,16,2048]{2,1,0:T(8,128)(2,1)}, u32[]{:S(2)}, u32[]{:S(2)}) async-start(bf16[64,16,2048]{2,1,0:T(8,128)(2,1)} %bitcast.39), calls=%async_computation.1 | async-start | bytes 8388608 | tf_op jit(solution)/shard_map/all_to_all | solution.py:72
  152.7 59.9 %reduce-scatter.4.cloned.1.call-start = ((), (), s32[]{:S(2)}) async-start(), calls=%async_computation.4 | async-start | bytes 2654208
Sparse Core Ops, SparseCore 0:
  34.8 48.5 all-gather.1
  161.6 50.9 reduce-scatter.3
where the time goes:
time: 269 us; the launch traced here: 268 us
  waiting for transfers between devices  180 us (67%)
  matrix products  24.8 us (9%)
  local copies, waits for them, and re-layouts  19.8 us (7%)
  starting transfers between devices  17 us (6%)
  between operations  14.2 us (5%)
  other arithmetic  12.9 us (5%)
    all_gather x1, waiting for transfers between devices, local(): weights = lax.all_gather(weights, 'dp', axis=0, tiled=True)  51.1 us
    unnamed x3, waiting for transfers between devices  50.9 us
    all_to_all x1, waiting for transfers between devices, local(): lax.all_to_all(send, 'expert', split_axis=0, concat_axis=0, tiled=True)  44.2 us
    all_to_all x1, waiting for transfers between devices, local(): lax.all_to_all(jnp.concatenate([expert_out, grad_in], axis=1), 'expert',...  33.5 us
    all_to_all x1, starting transfers between devices, local(): lax.all_to_all(send, 'expert', split_axis=0, concat_axis=0, tiled=True)  11.1 us
    unnamed x13, local copies, waits for them, and re-layouts  8.95 us
    concatenate x1, local copies, waits for them, and re-layouts, local(): jnp.concatenate([expert_out, grad_in], axis=1)  6.49 us
    all_to_all x1, starting transfers between devices, local(): lax.all_to_all(jnp.concatenate([expert_out, grad_in], axis=1), 'expert',...  5.88 us
  transfers between devices with their start and end apart: 4, of which 4 were waited for; matrix products, arithmetic and copies ran while one was open for 5% of the time, Pallas kernels for 0%

commit v1 on v0

--- a/solution.py
+++ b/solution.py
@@ -42,7 +42,22 @@
     slot_count = expert_count * capacity
     gate_width = gate_up.shape[2]
     weights = jnp.concatenate([gate_up[0], down_proj[0].T], axis=1)
-    weights = lax.all_gather(weights, "dp", axis=0, tiled=True)
+    res, b_now, everything = (lax.axis_size("dp"), lax.axis_index("dp"), weights.shape[0])
+    rows = [(src_i, (src_i + 1) % res) for src_i in range(res)]
+    big = jnp.zeros((*weights.shape[:0], res * everything, *weights.shape[1:]), weights.dtype)
+    big = lax.dynamic_update_slice_in_dim(big, weights, b_now * everything, axis=0)
+    made = [(src_i, (src_i - 1) % res) for src_i in range(res)]
+    v_next = block_now = weights
+    v1 = res // 2
+    for w in [*range(1, v1 + 1)]:
+        v_next = lax.ppermute(v_next, axis_name="dp", perm=rows)
+        big = lax.dynamic_update_slice_in_dim(big, v_next, (b_now - w) % res * everything, axis=0)
+        if w < res - v1:
+            block_now = lax.ppermute(block_now, axis_name="dp", perm=made)
+            big = lax.dynamic_update_slice_in_dim(
+                big, block_now, (b_now + w) % res * everything, axis=0
+            )
+    weights = big
     weight_in = weights[:, :gate_width]
     weight_out_t = weights[:, gate_width:]
     flat_ids = expert_ids.reshape(route_count)

time: 269 us -> 269 us (level)
  waiting for transfers between devices: 180 us -> 147 us
  starting transfers between devices: 17 us -> 46.1 us
    all_gather x1 -> x0, waiting for transfers between devices: 51.1 us -> none  [local(): weights = lax.all_gather(weights, 'dp', axis=0, tiled=True)]
    ppermute x0 -> x7, starting transfers between devices: none -> 29 us  [the longest x3 18.9 us: local(): block_now = lax.ppermute(block_now, axis_name='dp', perm=made)]
    ppermute x0 -> x7, waiting for transfers between devices: none -> 19.5 us  [the longest x4 19.5 us: local(): v_next = lax.ppermute(v_next, axis_name='dp', perm=rows)]
    unnamed x13 -> x21, local copies, waits for them, and re-layouts: 8.95 us -> 9.07 us
    unnamed x3 -> x2, waiting for transfers between devices: 50.9 us -> 50.8 us
  transfers between devices with their start and end apart: 4 -> 10, of which waited for: 4 -> 7; matrix products, arithmetic and copies ran while one was open for 5% -> 6% of each run, Pallas kernels for 0% -> 0%
where the time goes in v1:
time: 269 us; the launch traced here: 268 us
  waiting for transfers between devices  147 us (55%)
  starting transfers between devices  46.1 us (17%)
  matrix products  24.3 us (9%)
  local copies, waits for them, and re-layouts  22.3 us (8%)
  between operations  14.5 us (5%)
  other arithmetic  13.1 us (5%)
    unnamed x2, waiting for transfers between devices  50.8 us
    all_to_all x1, waiting for transfers between devices, local(): lax.all_to_all(send, 'expert', split_axis=0, concat_axis=0, tiled=True)  44 us
    all_to_all x1, waiting for transfers between devices, local(): lax.all_to_all(jnp.concatenate([expert_out, grad_in], axis=1), 'expert',...  33.1 us
    ppermute x4, waiting for transfers between devices, local(): v_next = lax.ppermute(v_next, axis_name='dp', perm=rows)  19.5 us
    ppermute x3, starting transfers between devices, local(): block_now = lax.ppermute(block_now, axis_name='dp', perm=made)  18.9 us
    all_to_all x1, starting transfers between devices, local(): lax.all_to_all(send, 'expert', split_axis=0, concat_axis=0, tiled=True)  11 us
    ppermute x4, starting transfers between devices, local(): v_next = lax.ppermute(v_next, axis_name='dp', perm=rows)  10.1 us
    unnamed x21, local copies, waits for them, and re-layouts  9.07 us
  transfers between devices with their start and end apart: 10, of which 7 were waited for; matrix products, arithmetic and copies ran while one was open for 6% of the time, Pallas kernels for 0%

profile of v1, /device:TPU:2, one launch (start us, length us, event | category | flops | bytes accessed | tf_op | source)
XLA Modules:
  0.0 267.8 jit_solution(472551911405040846)
XLA Ops:
  7.2 0.8 copy.46
  8.0 0.1 eq.50
  8.1 0.1 eq.46
  8.2 1.2 reduce-window.6
  9.4 0.2 slice_reduce_fusion
  9.7 0.1 fusion.36
  9.8 0.1 reduce_sum.39
  9.9 0.1 copy.49
  10.0 0.7 compare_select_fusion
  10.7 0.4 fusion.2
  11.0 1.0 select_reduce_fusion
  12.1 2.3 fusion.30
  14.3 0.3 slice.115
  14.7 2.9 %copy-done = f32[1024,2048]{1,0:T(8,128)} copy-done((f32[1024,2048]{1,0:T(8,128)}, f32[1024,2048]{1,0:T(8,128)S(1)}, u32[]{:S(2)}) %copy-start) | copy-done | bytes 8388632
  17.6 0.3 multiply_convert_fusion
  17.9 2.4 pad_maximum_fusion
  20.3 11.0 %all-to-all-start = ((bf16[64,16,2048]{2,1,0:T(8,128)(2,1)}), bf16[64,16,2048]{2,1,0:T(8,128)(2,1)}, u32[]{:S(2)}, u32[]{:S(2)}) async-start(bf16[64,16,2048]{2,1,0:T(8,128)(2,1)} %bitcast.39), calls=%async_computation | async-start | bytes 8388608 | tf_op jit(solution)/shard_map/all_to_all | solution.py:81
  31.3 0.1 copy.50
  31.5 0.2 broadcast_in_dim.30
  31.6 1.0 pad_maximum_fusion.6
  32.6 4.2 %collective-permute-start = (bf16[128,1152]{1,0:T(8,128)(2,1)S(1)}, bf16[128,1152]{1,0:T(8,128)(2,1)}, u32[]{:S(2)}, u32[]{:S(2)}) collective-permute-start(bf16[128,1152]{1,0:T(8,128)(2,1)S(1)} %get-tuple-element.37), channel_id=1, source_target_pairs={{0,64},{64,128},{128,192},{192,256},{256,320},{320,384},{384,448},... | collective-permute-start | bytes 884744 | tf_op jit(solution)/shard_map/ppermute | solution.py:53
  36.8 8.6 %collective-permute-start.1 = (bf16[128,1152]{1,0:T(8,128)(2,1)S(1)}, bf16[128,1152]{1,0:T(8,128)(2,1)}, u32[]{:S(2)}, u32[]{:S(2)}) collective-permute-start(bf16[128,1152]{1,0:T(8,128)(2,1)S(1)} %get-tuple-element.37), channel_id=1, source_target_pairs={{0,448},{64,0},{128,64},{192,128},{256,192},{320,256},{384,320},{4... | collective-permute-start | bytes 884744 | tf_op jit(solution)/shard_map/ppermute | solution.py:56
  45.6 5.3 %collective-permute-done = bf16[128,1152]{1,0:T(8,128)(2,1)} collective-permute-done((bf16[128,1152]{1,0:T(8,128)(2,1)S(1)}, bf16[128,1152]{1,0:T(8,128)(2,1)}, u32[]{:S(2)}, u32[]{:S(2)}) %collective-permute-start) | collective-permute-done | bytes 294944 | tf_op jit(solution)/shard_map/ppermute | solution.py:53
  50.9 1.9 collective-permute-start.2
  52.8 0.0 collective-permute-done.1
  52.8 5.1 %collective-permute-start.3 = (bf16[128,1152]{1,0:T(8,128)(2,1)}, bf16[128,1152]{1,0:T(8,128)(2,1)S(1)}, u32[]{:S(2)}, u32[]{:S(2)}) collective-permute-start(bf16[128,1152]{1,0:T(8,128)(2,1)} %collective-permute-done.1), channel_id=1, source_target_pairs={{0,448},{64,0},{128,64},{192,128},{256,192},{320,256},{384,320},{4... | collective-permute-start | bytes 884744 | tf_op jit(solution)/shard_map/ppermute | solution.py:56
  57.9 1.0 constant_dynamic-update-slice_fusion.6
  58.9 1.0 constant_dynamic-update-slice_fusion.5
  59.9 2.7 %collective-permute-done.2 = bf16[128,1152]{1,0:T(8,128)(2,1)S(1)} collective-permute-done((bf16[128,1152]{1,0:T(8,128)(2,1)}, bf16[128,1152]{1,0:T(8,128)(2,1)S(1)}, u32[]{:S(2)}, u32[]{:S(2)}) %collective-permute-start.2) | collective-permute-done | bytes 294944 | tf_op jit(solution)/shard_map/ppermute | solution.py:53
  62.6 1.9 collective-permute-start.4
  64.6 0.0 collective-permute-done.3
  64.6 5.1 %collective-permute-start.5 = (bf16[128,1152]{1,0:T(8,128)(2,1)S(1)}, bf16[128,1152]{1,0:T(8,128)(2,1)S(1)}, u32[]{:S(2)}, u32[]{:S(2)}) collective-permute-start(bf16[128,1152]{1,0:T(8,128)(2,1)S(1)} %collective-permute-done.3), channel_id=1, source_target_pairs={{0,448},{64,0},{128,64},{192,128},{256,192},{320,256},{384,320},{4... | collective-permute-start | bytes 884744 | tf_op jit(solution)/shard_map/ppermute | solution.py:56
  69.8 3.6 %collective-permute-done.4 = bf16[128,1152]{1,0:T(8,128)(2,1)S(1)} collective-permute-done((bf16[128,1152]{1,0:T(8,128)(2,1)S(1)}, bf16[128,1152]{1,0:T(8,128)(2,1)S(1)}, u32[]{:S(2)}, u32[]{:S(2)}) %collective-permute-start.4) | collective-permute-done | bytes 294944 | tf_op jit(solution)/shard_map/ppermute | solution.py:53
  73.4 2.1 collective-permute-start.6
  75.6 0.0 collective-permute-done.5
  75.6 7.8 %collective-permute-done.6 = bf16[128,1152]{1,0:T(8,128)(2,1)S(1)} collective-permute-done((bf16[128,1152]{1,0:T(8,128)(2,1)S(1)}, bf16[128,1152]{1,0:T(8,128)(2,1)S(1)}, u32[]{:S(2)}, u32[]{:S(2)}) %collective-permute-start.6) | collective-permute-done | bytes 294944 | tf_op jit(solution)/shard_map/ppermute | solution.py:53
  83.5 44.0 %all-to-all-done = bf16[64,16,2048]{2,1,0:T(8,128)(2,1)} async-done(((bf16[64,16,2048]{2,1,0:T(8,128)(2,1)}), bf16[64,16,2048]{2,1,0:T(8,128)(2,1)}, u32[]{:S(2)}, u32[]{:S(2)}) %all-to-all-start) | async-done | bytes 4194336 | tf_op jit(solution)/shard_map/all_to_all | solution.py:81
  127.5 3.5 %fusion.11 = f32[1024,768]{0,1:T(8,128)S(1)} fusion(bf16[1024,2048]{1,0:T(8,128)(2,1)} %bitcast.2, bf16[1024,1152]{1,0:T(8,128)(2,1)S(1)} %constant_dynamic-update-slice_fusion), kind=kOutput, calls=%fused_computation.23 | convolution fusion | flops 1610612736 | bytes 6815744 | tf_op jit(solution)/shard_map/dot_general | solution.py:11
  131.0 3.3 %multiply_convert_fusion.2 = (bf16[1024,384]{0,1:T(8,128)(2,1)S(1)}, bf16[1024,384]{0,1:T(8,128)(2,1)S(1)}, bf16[1024,384]{0,1:T(8,128)(2,1)S(1)}) fusion(f32[1024,768]{0,1:T(8,128)S(1)} %fusion.11, bf16[1024,1152]{1,0:T(8,128)(2,1)S(1)} %constant_dynamic-update-slice_fusion, bf16[1024,2048]{1,0:T(8,128)(2,1)} %bitcast.2), kind=kOutput, calls=%fused_computation.28 | convolution fusion | flops 811204608 | bytes 8388608 | tf_op jit(solution)/shard_map/dot_general | solution.py:19
  134.3 1.3 convolution_convert_fusion
  135.6 0.1 copy-done.6
  135.7 1.8 convolution_convert_fusion.1
  137.5 2.4 pad_maximum_fusion.1
  139.9 6.5 %copy.51 = bf16[1024,2048]{1,0:T(8,128)(2,1)} copy(bf16[1024,2048]{0,1:T(8,128)(2,1)} %pad_maximum_fusion.1) | data formatting | bytes 8388608 | tf_op jit(solution)/shard_map/concatenate | solution.py:88
  146.4 5.8 %all-to-all-start.1 = ((bf16[64,16,2048]{2,1,0:T(8,128)(2,1)}), bf16[64,16,2048]{2,1,0:T(8,128)(2,1)}, u32[]{:S(2)}, u32[]{:S(2)}) async-start(bf16[64,16,2048]{2,1,0:T(8,128)(2,1)} %bitcast.40), calls=%async_computation.1 | async-start | bytes 8388608 | tf_op jit(solution)/shard_map/all_to_all | solution.py:87
  152.2 0.3 reduce-scatter.4.cloned.1.call-start
  152.5 2.7 %fusion.17 = bf16[1024,384]{0,1:T(8,128)(2,1)S(1)} fusion(bf16[1024,384]{0,1:T(8,128)(2,1)S(1)} %copy-done.3, bf16[1024,2048]{1,0:T(8,128)(2,1)} %bitcast.2), kind=kOutput, calls=%fused_computation.32 | convolution fusion | flops 805699584 | bytes 3670016 | tf_op jit(solution)/shard_map/dot_general | solution.py:30
  155.2 3.4 %fusion.13 = bf16[1024,768]{0,1:T(8,128)(2,1)S(1)} fusion(bf16[1024,2048]{1,0:T(8,128)(2,1)} %bitcast.2, bf16[1024,384]{0,1:T(8,128)(2,1)S(1)} %copy-done.7, bf16[1024,384]{0,1:T(8,128)(2,1)S(1)} %copy-done.5), kind=kOutput, calls=%fused_computation.25 | convolution fusion | flops 1614544896 | bytes 5242880 | tf_op jit(solution)/shard_map/dot_general | solution.py:27
  158.6 0.2 pad_maximum_fusion.2
  158.9 2.5 copy.55
  161.4 0.0 reduce-scatter.4.cloned.1.call-update
  161.4 0.1 copy.52
  161.5 0.1 reshape.45
  161.6 50.8 %reduce-scatter.4.cloned.1.call-done = bf16[128,1152]{1,0:T(8,128)(2,1)} async-done(((bf16[1024,1152]{1,0:T(8,128)(2,1)}), bf16[128,1152]{1,0:T(8,128)(2,1)}) %reduce-scatter.4.cloned.1.call-update) | async-done | bytes 294928
  212.4 1.2 copy.56
  213.7 0.9 copy.54
  214.6 0.7 slice_bitcast_fusion.1
  215.3 33.1 %all-to-all-done.1 = bf16[64,16,2048]{2,1,0:T(8,128)(2,1)} async-done(((bf16[64,16,2048]{2,1,0:T(8,128)(2,1)}), bf16[64,16,2048]{2,1,0:T(8,128)(2,1)}, u32[]{:S(2)}, u32[]{:S(2)}) %all-to-all-start.1) | async-done | bytes 4194336 | tf_op jit(solution)/shard_map/all_to_all | solution.py:87
  248.4 3.3 %multiply_reduce_fusion = f32[1024]{0:T(1024)S(1)} fusion(f32[1024,2048]{1,0:T(8,128)} %copy-done, bf16[1024,2048]{1,0:T(8,128)(2,1)} %bitcast.7), kind=kLoop, calls=%fused_computation.4 | loop fusion | flops 3144704 | bytes 6295552 | tf_op jit(solution)/shard_map/reduce_sum | solution.py:114
  251.7 2.8 %fusion.25 = bf16[128,1024]{1,0:T(8,128)(2,1)} fusion(pred[1024,128]{1,0:T(8,128)(4,1)S(1)} %fusion.2, bf16[1024,2048]{1,0:T(8,128)(2,1)} %bitcast.7), kind=kOutput, calls=%fused_computation.36 | convolution fusion | flops 268566528 | bytes 2490368 | tf_op jit(solution)/shard_map/dot_general | solution.py:111
  254.5 2.3 gather_fusion
  256.8 0.1 reshape.44
  256.9 0.7 copy.53
  257.6 3.4 %fusion.22 = bf16[128,1024]{1,0:T(8,128)(2,1)} fusion(f32[1024,128]{1,0:T(8,128)S(1)} %get-tuple-element.31, bf16[1024,2048]{1,0:T(8,128)(2,1)} %bitcast.7), kind=kOutput, calls=%fused_computation.35 | convolution fusion | flops 1610743808 | bytes 2883584 | tf_op jit(solution)/shard_map/dot_general | solution.py:104
  (25 shorter events, 0.3 us)
Async XLA Ops:
  14.3 3.2 %copy-start = (f32[1024,2048]{1,0:T(8,128)}, f32[1024,2048]{1,0:T(8,128)S(1)}, u32[]{:S(2)}) copy-start(f32[1024,2048]{1,0:T(8,128)S(1)} %fusion.30) | copy-start | bytes 25165828
  20.3 11.1 %copy-start.1 = (bf16[1,384,128]{2,1,0:T(8,128)(2,1)S(1)}, bf16[1,384,128]{2,1,0:T(8,128)(2,1)}, u32[]{:S(2)}) copy-start(bf16[1,384,128]{2,1,0:T(8,128)(2,1)} %param.10) | copy-start | bytes 294916
  20.3 107.3 %all-to-all-start = ((bf16[64,16,2048]{2,1,0:T(8,128)(2,1)}), bf16[64,16,2048]{2,1,0:T(8,128)(2,1)}, u32[]{:S(2)}, u32[]{:S(2)}) async-start(bf16[64,16,2048]{2,1,0:T(8,128)(2,1)} %bitcast.39), calls=%async_computation | async-start | bytes 8388608 | tf_op jit(solution)/shard_map/all_to_all | solution.py:81
  32.6 18.3 %collective-permute-start = (bf16[128,1152]{1,0:T(8,128)(2,1)S(1)}, bf16[128,1152]{1,0:T(8,128)(2,1)}, u32[]{:S(2)}, u32[]{:S(2)}) collective-permute-start(bf16[128,1152]{1,0:T(8,128)(2,1)S(1)} %get-tuple-element.37), channel_id=1, source_target_pairs={{0,64},{64,128},{128,192},{192,256},{256,320},{320,384},{384,448},... | collective-permute-start | bytes 884744 | tf_op jit(solution)/shard_map/ppermute | solution.py:53
  36.8 16.0 %collective-permute-start.1 = (bf16[128,1152]{1,0:T(8,128)(2,1)S(1)}, bf16[128,1152]{1,0:T(8,128)(2,1)}, u32[]{:S(2)}, u32[]{:S(2)}) collective-permute-start(bf16[128,1152]{1,0:T(8,128)(2,1)S(1)} %get-tuple-element.37), channel_id=1, source_target_pairs={{0,448},{64,0},{128,64},{192,128},{256,192},{320,256},{384,320},{4... | collective-permute-start | bytes 884744 | tf_op jit(solution)/shard_map/ppermute | solution.py:56
  50.9 11.8 %collective-permute-start.2 = (bf16[128,1152]{1,0:T(8,128)(2,1)}, bf16[128,1152]{1,0:T(8,128)(2,1)S(1)}, u32[]{:S(2)}, u32[]{:S(2)}) collective-permute-start(bf16[128,1152]{1,0:T(8,128)(2,1)} %collective-permute-done), channel_id=1, source_target_pairs={{0,64},{64,128},{128,192},{192,256},{256,320},{320,384},{384,448},... | collective-permute-start | bytes 884744 | tf_op jit(solution)/shard_map/ppermute | solution.py:53
  52.8 11.7 %collective-permute-start.3 = (bf16[128,1152]{1,0:T(8,128)(2,1)}, bf16[128,1152]{1,0:T(8,128)(2,1)S(1)}, u32[]{:S(2)}, u32[]{:S(2)}) collective-permute-start(bf16[128,1152]{1,0:T(8,128)(2,1)} %collective-permute-done.1), channel_id=1, source_target_pairs={{0,448},{64,0},{128,64},{192,128},{256,192},{320,256},{384,320},{4... | collective-permute-start | bytes 884744 | tf_op jit(solution)/shard_map/ppermute | solution.py:56
  62.6 10.8 %collective-permute-start.4 = (bf16[128,1152]{1,0:T(8,128)(2,1)S(1)}, bf16[128,1152]{1,0:T(8,128)(2,1)S(1)}, u32[]{:S(2)}, u32[]{:S(2)}) collective-permute-start(bf16[128,1152]{1,0:T(8,128)(2,1)S(1)} %collective-permute-done.2), channel_id=1, source_target_pairs={{0,64},{64,128},{128,192},{192,256},{256,320},{320,384},{384,448},... | collective-permute-start | bytes 884744 | tf_op jit(solution)/shard_map/ppermute | solution.py:53
  64.6 11.0 %collective-permute-start.5 = (bf16[128,1152]{1,0:T(8,128)(2,1)S(1)}, bf16[128,1152]{1,0:T(8,128)(2,1)S(1)}, u32[]{:S(2)}, u32[]{:S(2)}) collective-permute-start(bf16[128,1152]{1,0:T(8,128)(2,1)S(1)} %collective-permute-done.3), channel_id=1, source_target_pairs={{0,448},{64,0},{128,64},{192,128},{256,192},{320,256},{384,320},{4... | collective-permute-start | bytes 884744 | tf_op jit(solution)/shard_map/ppermute | solution.py:56
  73.4 10.0 %collective-permute-start.6 = (bf16[128,1152]{1,0:T(8,128)(2,1)S(1)}, bf16[128,1152]{1,0:T(8,128)(2,1)S(1)}, u32[]{:S(2)}, u32[]{:S(2)}) collective-permute-start(bf16[128,1152]{1,0:T(8,128)(2,1)S(1)} %collective-permute-done.4), channel_id=1, source_target_pairs={{0,64},{64,128},{128,192},{192,256},{256,320},{320,384},{384,448},... | collective-permute-start | bytes 884744 | tf_op jit(solution)/shard_map/ppermute | solution.py:53
  134.2 1.3 copy-start.2
  134.3 1.3 copy-start.4
  134.3 1.4 copy-start.6
  146.4 6.1 %copy-start.3 = (bf16[1024,384]{0,1:T(8,128)(2,1)S(1)}, bf16[1024,384]{0,1:T(8,128)(2,1)}, u32[]{:S(2)}) copy-start(bf16[1024,384]{0,1:T(8,128)(2,1)} %copy-done.2) | copy-start | bytes 2359300
  146.4 102.0 %all-to-all-start.1 = ((bf16[64,16,2048]{2,1,0:T(8,128)(2,1)}), bf16[64,16,2048]{2,1,0:T(8,128)(2,1)}, u32[]{:S(2)}, u32[]{:S(2)}) async-start(bf16[64,16,2048]{2,1,0:T(8,128)(2,1)} %bitcast.40), calls=%async_computation.1 | async-start | bytes 8388608 | tf_op jit(solution)/shard_map/all_to_all | solution.py:87
  152.2 3.0 %copy-start.5 = (bf16[1024,384]{0,1:T(8,128)(2,1)S(1)}, bf16[1024,384]{0,1:T(8,128)(2,1)}, u32[]{:S(2)}) copy-start(bf16[1024,384]{0,1:T(8,128)(2,1)} %copy-done.4) | copy-start | bytes 2359300
  152.2 3.0 %copy-start.7 = (bf16[1024,384]{0,1:T(8,128)(2,1)S(1)}, bf16[1024,384]{0,1:T(8,128)(2,1)}, u32[]{:S(2)}) copy-start(bf16[1024,384]{0,1:T(8,128)(2,1)} %copy-done.6) | copy-start | bytes 2359300
  152.2 60.2 %reduce-scatter.4.cloned.1.call-start = ((), (), s32[]{:S(2)}) async-start(), calls=%async_computation.3 | async-start | bytes 2654208
Sparse Core Ops, SparseCore 0:
  161.5 50.8 reduce-scatter.3
